TPU v7x, 128 devices: a whole 4x4x4 slice. The times are simulated.
128 devices in a mesh: ang: 64 (over x, y_lo, z, core), pix: 2 (over y_hi).
Axes of the slice: x: 4, y: 4 (y_hi: 2, y_lo: 2; y = y_hi * 2 + y_lo), z: 4, core: 2. Of those that a mesh axis runs over, the one named last changes fastest.
Arguments:
- grads: bfloat16 [2, 4096, 128, 512], P(None, 'ang', 'pix')
- circle_pos: int32 [4096], replicated, may hold values from 0 to 4095, as said below
- harmonics: int32 [256], replicated, may hold values from 0 to 4095, as said below
- support: int32 [128, 512], replicated, may hold values 0 or 1
Outputs:
- update: bfloat16 [2, 4096, 128, 512], P(None, 'ang', 'pix')
- harmonic_rms: float32 [256], replicated
Inputs may be any that keep to these rules, and one draw needn't show every extreme that they name: `circle_pos`: the stored angles form 64 aligned blocks of 64 rows; block b holds the circle positions r_b + 64 * j for j = 0 to 63 in this order, and the 64 values r_b are distinct. `harmonics`: 256 distinct harmonic numbers, among them 0 and 4095.
All inputs are finite; a program needn't handle non-finite values.
Results may differ from a plain program's by a relative error of at most 0.015.
Values may be sent and summed in bfloat16 or wider, within the bound.
No kernel may reach another device: no remote copies, remote signals or barrier semaphores. Data moves between devices by JAX's collectives and lax.ppermute only.
A program may use at most 192 MiB of HBM per device.

v0:
```python
import math
import jax
import jax.numpy as jnp
from jax import lax
from jax.sharding import PartitionSpec as P


def phase_pair(product, modulus):
    radians = (product % modulus).astype(jnp.float32) * (2.0 * math.pi / modulus)
    return (jnp.cos(radians), jnp.sin(radians))


def split_parts(value):
    if value.dtype == jnp.bfloat16:
        return (value,)
    high = value.astype(jnp.bfloat16)
    low = (value - high.astype(jnp.float32)).astype(jnp.bfloat16)
    return (high, low)


def split_einsum(form, left, right):
    left_parts = split_parts(left)
    right_parts = split_parts(right)
    total = None
    for left_rank, left_piece in enumerate(left_parts):
        for right_rank, right_piece in enumerate(right_parts):
            if left_rank + right_rank <= 1:
                term = jnp.einsum(form, left_piece, right_piece, preferred_element_type=jnp.float32)
                total = term if total is None else total + term
    return total


def normalize(coef_re, coef_im, weight, cell_count):
    square_sums = jnp.sum(weight[None, :] * (coef_re * coef_re + coef_im * coef_im), axis=1)
    totals = lax.psum(square_sums, ("ang", "pix"))
    harmonic_rms = jnp.sqrt(totals / cell_count + 1e-06)
    factor = weight[None, :] / harmonic_rms[:, None]
    return (coef_re * factor, coef_im * factor, harmonic_rms)


def direct_path(grads, circle_pos, harmonics, weight, cell_count):
    angle_count = circle_pos.shape[0]
    kept_count = harmonics.shape[0]
    moved = lax.all_to_all(grads, "ang", split_axis=2, concat_axis=1, tiled=True)
    row_local = moved.shape[2]
    col_count = moved.shape[3]
    flat = moved.reshape(2, angle_count, row_local * col_count)
    pixel_count = flat.shape[2]
    phase_cos, phase_sin = phase_pair(harmonics[:, None] * circle_pos[None, :], angle_count)
    table = jnp.concatenate((phase_cos, phase_sin), 0)
    products = split_einsum("ka,ap->kp", table, jnp.concatenate((flat[0], flat[1]), 1))
    scale = 1.0 / math.sqrt(angle_count)
    coef_re = (products[:kept_count, :pixel_count] + products[kept_count:, pixel_count:]) * scale
    coef_im = (products[:kept_count, pixel_count:] - products[kept_count:, :pixel_count]) * scale
    step_re, step_im, harmonic_rms = normalize(coef_re, coef_im, weight, cell_count)
    right_side = jnp.concatenate(
        (jnp.concatenate((step_re, -step_im), 0), jnp.concatenate((step_im, step_re), 0)), 1
    )
    synthesis = split_einsum("ka,kp->ap", table, right_side)
    scale_back = 1.0 / math.sqrt(kept_count)
    update = jnp.stack((synthesis[:, :pixel_count], synthesis[:, pixel_count:])) * scale_back
    update = update.astype(jnp.bfloat16).reshape(2, angle_count, row_local, col_count)
    return (lax.all_to_all(update, "ang", split_axis=1, concat_axis=2, tiled=True), harmonic_rms)


def body(grads, circle_pos, harmonics, support):
    ang_count = lax.axis_size("ang")
    row_pix = grads.shape[2]
    row_local = row_pix // ang_count
    col_count = grads.shape[3]
    row_start = lax.axis_index("pix") * row_pix + lax.axis_index("ang") * row_local
    weight = (
        lax.dynamic_slice_in_dim(support, row_start, row_local, 0).astype(jnp.float32).reshape(-1)
    )
    cell_count = float(row_pix * lax.axis_size("pix") * col_count)
    update, harmonic_rms = direct_path(grads, circle_pos, harmonics, weight, cell_count)
    return (update, harmonic_rms)


def solution(mesh):
    placed = (P(None, "ang", "pix", None), P(), P(), P())
    return jax.shard_map(
        body,
        mesh=mesh,
        in_specs=placed,
        out_specs=(P(None, "ang", "pix", None), P()),
        check_vma=False,
    )
```

profile of v0, /device:TPU:1, one launch (start us, length us, event | category | flops | bytes accessed | tf_op | source)
XLA Modules:
  0.0 437.9 jit_solution(5942899219189294290)
XLA Ops:
  0.6 11.5 %copy.18 = bf16[2,64,64,512]{3,1,0,2:T(8,128)(2,1)} copy(bf16[2,64,64,512]{3,2,1,0:T(8,128)(2,1)} %param.4) | data formatting | bytes 16777216 | tf_op args[0]
  12.1 0.0 copy-start.6
  12.1 0.0 copy-start.8
  12.1 11.2 %all-to-all-start = ((bf16[2,64,64,512]{3,1,0,2:T(8,128)(2,1)}), bf16[2,64,64,512]{3,1,0,2:T(8,128)(2,1)}, u32[]{:S(2)}, u32[]{:S(2)}) async-start(bf16[2,64,64,512]{3,1,0,2:T(8,128)(2,1)} %copy.18), calls=%async_computation | async-start | bytes 16777216 | tf_op jit(solution)/shard_map/all_to_all | solution.py:44
  23.3 0.7 dynamic-slice_convert_fusion
  24.1 0.0 copy-done.6
  24.1 0.0 copy-done.8
  24.1 18.0 %fusion.8 = (f32[256,4096]{1,0:T(8,128)}, f32[256,4096]{1,0:T(8,128)}) fusion(s32[4096]{0:T(1024)S(1)} %copy-done.6, s32[256]{0:T(256)S(1)} %copy-done.8), kind=kLoop, calls=%fused_computation.23 | loop fusion | flops 14680064 | bytes 8406016 | tf_op jit(solution)/shard_map/cos | solution.py:10
  42.1 84.6 %all-to-all-done = bf16[2,64,64,512]{3,1,0,2:T(8,128)(2,1)} async-done(((bf16[2,64,64,512]{3,1,0,2:T(8,128)(2,1)}), bf16[2,64,64,512]{3,1,0,2:T(8,128)(2,1)}, u32[]{:S(2)}, u32[]{:S(2)}) %all-to-all-start) | async-done | bytes 8388640 | tf_op jit(solution)/shard_map/all_to_all | solution.py:44
  126.7 7.9 %copy.24 = bf16[2,64,64,512]{3,1,2,0:T(8,128)(2,1)} copy(bf16[2,64,64,512]{3,1,0,2:T(8,128)(2,1)} %all-to-all-done) | data formatting | bytes 16777216 | tf_op jit(solution)/shard_map/all_to_all | solution.py:44
  134.6 0.0 copy-start
  134.6 0.0 copy-start.2
  134.6 5.4 %fusion.27 = (bf16[1,64,64,1,512]{4,2,1,3,0:T(8,128)(2,1)S(1)}, bf16[1,64,64,1,512]{4,2,1,3,0:T(8,128)(2,1)}) fusion(bf16[2,64,64,1,512]{4,2,1,3,0:T(8,128)(2,1)} %bitcast.17), kind=kLoop, calls=%fused_computation.41 | loop fusion | bytes 16777216 | tf_op jit(solution)/shard_map/slice | solution.py:51
  140.0 0.0 copy-start.5
  140.0 2.1 copy-done.5
  142.1 0.0 copy-done
  142.1 1.5 copy-done.2
  143.6 8.0 %fusion.2 = f32[512,1024]{1,0:T(8,128)} fusion(bf16[4096,512]{1,0:T(8,128)(2,1)} %bitcast.21, bf16[4096,512]{1,0:T(8,128)(2,1)S(1)} %bitcast.19, f32[256,4096]{1,0:T(8,128)S(1)} %copy-done.2, f32[256,4096]{1,0:T(8,128)S(1)} %copy-done), kind=kOutput, calls=%fused_computation.15 | convolution fusion | flops 4322230272 | bytes 18874368 | tf_op jit(solution)/shard_map/ka,ap->kp/dot_general | solution.py:28
  151.6 8.5 %fusion.9 = f32[512,1024]{1,0:T(8,128)S(1)} fusion(f32[512,1024]{1,0:T(8,128)} %fusion.2, bf16[4096,512]{1,0:T(8,128)(2,1)} %bitcast.22, bf16[4096,512]{1,0:T(8,128)(2,1)} %bitcast.20, f32[256,4096]{1,0:T(8,128)S(1)} %copy-done.2, f32[256,4096]{1,0:T(8,128)S(1)} %copy-done), kind=kOutput, calls=%fused_computation.24 | convolution fusion | flops 4320657408 | bytes 20971520 | tf_op jit(solution)/shard_map/ka,ap->kp/dot_general | solution.py:28
  160.1 0.0 copy-start.4
  160.2 1.3 copy-done.4
  161.5 0.2 multiply_reduce_fusion
  161.7 70.5 %psum.7 = f32[256]{0:T(256)S(1)} all-reduce(f32[256]{0:T(256)S(1)} %multiply_reduce_fusion), channel_id=1, replica_groups=mesh['ang'=64,'pix'=2] {'ang','pix'}, use_global_device_ids=true, to_apply=%region_1.2 | all-reduce | flops 256 | bytes 2048 | tf_op jit(solution)/shard_map/psum | solution.py:35
  232.2 0.0 copy-start.7
  232.3 1.7 fusion.26
  234.0 0.0 copy-start.1
  234.0 0.0 copy-start.3
  234.0 12.7 %fusion.11 = f32[4096,1024]{1,0:T(8,128)} fusion(f32[256,512]{1,0:T(8,128)S(1)} %get-tuple-element.12, f32[256,512]{1,0:T(8,128)S(1)} %get-tuple-element.7, f32[256,512]{1,0:T(8,128)S(1)} %get-tuple-element.6, f32[256,4096]{1,0:T(8,128)} %get-tuple-element.14, f32[256,4096]{1,0:T(8,128)} %get-tuple-element.13), kind=kOutput, calls=%fused_computation.26 | convolution fusion | flops 4307025920 | bytes 26738688 | tf_op jit(solution)/shard_map/ka,kp->ap/dot_general | solution.py:28
  246.7 0.0 copy-done.7
  246.7 0.0 copy-done.1
  246.7 0.0 copy-done.3
  246.7 8.2 %fusion.19 = f32[4096,1024]{1,0:T(8,128)} fusion(f32[256,512]{1,0:T(8,128)S(1)} %get-tuple-element.12, f32[256,512]{1,0:T(8,128)S(1)} %get-tuple-element.7, f32[256,512]{1,0:T(8,128)S(1)} %get-tuple-element.6, f32[256,4096]{1,0:T(8,128)S(1)} %copy-done.3, f32[256,4096]{1,0:T(8,128)S(1)} %copy-done.1), kind=kOutput, calls=%fused_computation.39 | convolution fusion | flops 4307550208 | bytes 26738688 | tf_op jit(solution)/shard_map/ka,kp->ap/dot_general | solution.py:28
  254.9 19.3 %add_add_fusion = f32[4096,1024]{1,0:T(8,128)} fusion(f32[4096,1024]{1,0:T(8,128)} %fusion.19, f32[4096,1024]{1,0:T(8,128)} %fusion.11, f32[256,512]{1,0:T(8,128)S(1)} %get-tuple-element.12, f32[256,512]{1,0:T(8,128)S(1)} %get-tuple-element.7, f32[256,512]{1,0:T(8,128)S(1)} %get-tuple-element.6, f32[256,4096]{1,0:T(8,128)} %get-tuple-element.14, ...), kind=kOutput, calls=%fused_computation.2 | convolution fusion | flops 4318035968 | bytes 60293120 | tf_op jit(solution)/shard_map/ka,kp->ap/dot_general | solution.py:28
  274.1 6.9 %slice_bitcast_fusion.1 = (f32[1,4096,1,512]{3,1,2,0:T(8,128)S(1)}, f32[1,4096,1,512]{3,1,2,0:T(8,128)S(1)}) fusion(f32[4096,1024]{1,0:T(8,128)} %add_add_fusion), kind=kLoop, calls=%fused_computation.4 | loop fusion | bytes 33554432 | tf_op jit(solution)/shard_map/stack | solution.py:61
  281.0 2.5 fusion
  283.5 32.6 %copy.20 = bf16[2,4096,1,512]{3,0,2,1:T(2,128)(2,1)S(1)} copy(bf16[2,4096,1,512]{3,1,2,0:T(8,128)(2,1)S(1)} %fusion) | data formatting | bytes 16777216 | tf_op jit(solution)/shard_map/convert_element_type | solution.py:62
  316.2 102.3 %all_to_all.33 = bf16[2,4096,1,512]{3,0,2,1:T(2,128)(2,1)} all-to-all(bf16[2,4096,1,512]{3,0,2,1:T(2,128)(2,1)S(1)} %copy.20), channel_id=1, replica_groups=mesh['ang'=64,'pix'=2] {'ang'}, dimensions={1} | all-to-all | bytes 16777216 | tf_op jit(solution)/shard_map/all_to_all | solution.py:63
  418.4 8.0 %copy.21 = bf16[2,4096,1,512]{3,1,0,2:T(8,128)(2,1)} copy(bf16[2,4096,1,512]{3,0,2,1:T(2,128)(2,1)} %all_to_all.33) | data formatting | bytes 16777216 | tf_op jit(solution)/shard_map/all_to_all | solution.py:63
  426.4 11.5 %copy.22 = bf16[2,64,64,512]{3,2,1,0:T(8,128)(2,1)} copy(bf16[2,64,64,512]{3,1,2,0:T(8,128)(2,1)} %bitcast.18) | data formatting | bytes 16777216
  (1 shorter events, 0.0 us)
Async XLA Ops:
  12.1 11.9 %copy-start.6 = (s32[4096]{0:T(1024)S(1)}, s32[4096]{0:T(1024)}, u32[]{:S(2)}) copy-start(s32[4096]{0:T(1024)} %param.5) | copy-start | bytes 49156
  12.1 11.9 %copy-start.8 = (s32[256]{0:T(256)S(1)}, s32[256]{0:T(256)}, u32[]{:S(2)}) copy-start(s32[256]{0:T(256)} %param.6) | copy-start | bytes 3076
  12.1 114.6 %all-to-all-start = ((bf16[2,64,64,512]{3,1,0,2:T(8,128)(2,1)}), bf16[2,64,64,512]{3,1,0,2:T(8,128)(2,1)}, u32[]{:S(2)}, u32[]{:S(2)}) async-start(bf16[2,64,64,512]{3,1,0,2:T(8,128)(2,1)} %copy.18), calls=%async_computation | async-start | bytes 16777216 | tf_op jit(solution)/shard_map/all_to_all | solution.py:44
  134.6 7.5 %copy-start = (f32[256,4096]{1,0:T(8,128)S(1)}, f32[256,4096]{1,0:T(8,128)}, u32[]{:S(2)}) copy-start(f32[256,4096]{1,0:T(8,128)} %get-tuple-element.13) | copy-start | bytes 12582916
  134.6 9.0 %copy-start.2 = (f32[256,4096]{1,0:T(8,128)S(1)}, f32[256,4096]{1,0:T(8,128)}, u32[]{:S(2)}) copy-start(f32[256,4096]{1,0:T(8,128)} %get-tuple-element.14) | copy-start | bytes 12582916
  140.0 2.1 copy-start.5
  160.1 1.3 copy-start.4
  232.2 14.4 %copy-start.7 = (f32[256]{0:T(256)}, f32[256]{0:T(256)S(1)}, u32[]{:S(2)}) copy-start(f32[256]{0:T(256)S(1)} %add_sqrt_fusion) | copy-start | bytes 3076
  234.0 12.7 %copy-start.1 = (f32[256,4096]{1,0:T(8,128)S(1)}, f32[256,4096]{1,0:T(8,128)}, u32[]{:S(2)}) copy-start(f32[256,4096]{1,0:T(8,128)} %get-tuple-element.13) | copy-start | bytes 12582916
  234.0 12.7 %copy-start.3 = (f32[256,4096]{1,0:T(8,128)S(1)}, f32[256,4096]{1,0:T(8,128)}, u32[]{:S(2)}) copy-start(f32[256,4096]{1,0:T(8,128)} %get-tuple-element.14) | copy-start | bytes 12582916
where the time goes:
time: 438 us
  blocking collectives  173 us (39%)
  local copies, waits for them, and re-layouts  88.7 us (20%)
  waiting for transfers between devices  84.6 us (19%)
  matrix products  56.7 us (13%)
  other arithmetic  23.2 us (5%)
  starting transfers between devices  11.2 us (3%)
    all_to_all x1, blocking collectives, direct_path(): lax.all_to_all(update, 'ang', split_axis=1, concat_axis=2, tiled=True)  102 us
    all_to_all x1, waiting for transfers between devices, direct_path(): lax.all_to_all(grads, 'ang', split_axis=2, concat_axis=1, tiled=True)  84.6 us
    psum x1, blocking collectives, normalize(): totals = lax.psum(square_sums, ('ang', 'pix'))  70.5 us
    dot_general x5, matrix products, split_einsum(): jnp.einsum(form, left_piece, right_piece, preferred_element_type=jnp.floa...  56.7 us
    convert_element_type x1, local copies, waits for them, and re-layouts, direct_path(): update.astype(jnp.bfloat16).reshape(2, angle_count, row_local, col_count)  32.6 us
    unnamed x20, local copies, waits for them, and re-layouts  28 us
    cos x1, other arithmetic, phase_pair(): return (jnp.cos(radians), jnp.sin(radians))  18 us
    all_to_all x1, starting transfers between devices, direct_path(): lax.all_to_all(grads, 'ang', split_axis=2, concat_axis=1, tiled=True)  11.2 us
  transfers between devices with their start and end apart: 1, of which 1 were waited for; matrix products, arithmetic and copies ran while one was open for 4% of the time, Pallas kernels for 0%

commit v1 on v0

--- a/solution.py
+++ b/solution.py
@@ -60,7 +60,13 @@
     scale_back = 1.0 / math.sqrt(kept_count)
     update = jnp.stack((synthesis[:, :pixel_count], synthesis[:, pixel_count:])) * scale_back
     update = update.astype(jnp.bfloat16).reshape(2, angle_count, row_local, col_count)
-    return (lax.all_to_all(update, "ang", split_axis=1, concat_axis=2, tiled=True), harmonic_rms)
+    return (
+        jnp.concatenate(
+            lax.all_to_all(jnp.stack(jnp.split(update, lax.axis_size("ang"), axis=1)), "ang", 0, 0),
+            axis=2,
+        ),
+        harmonic_rms,
+    )
 
 
 def body(grads, circle_pos, harmonics, support):

time: 438 us -> 402 us (0.918)
  local copies, waits for them, and re-layouts: 88.7 us -> 48.8 us
    convert_element_type x1 -> x0, local copies, waits for them, and re-layouts: 32.6 us -> none  [direct_path(): update.astype(jnp.bfloat16).reshape(2, angle_count, row_local, col_count)]
    all_to_all x1 -> x0, local copies, waits for them, and re-layouts: 7.96 us -> none  [direct_path(): lax.all_to_all(update, 'ang', split_axis=1, concat_axis=2, tiled=True)]
    unnamed x20 -> x83, local copies, waits for them, and re-layouts: 28 us -> 28.7 us
  transfers between devices with their start and end apart: 1 -> 1, of which waited for: 1 -> 1; matrix products, arithmetic and copies ran while one was open for 4% -> 5% of each run, Pallas kernels for 0% -> 0%
where the time goes in v1:
time: 402 us; the launch traced here: 401 us
  blocking collectives  173 us (43%)
  waiting for transfers between devices  84.6 us (21%)
  matrix products  56.7 us (14%)
  local copies, waits for them, and re-layouts  48.8 us (12%)
  other arithmetic  25.7 us (6%)
  starting transfers between devices  11.2 us (3%)
    all_to_all x1, blocking collectives, direct_path(): lax.all_to_all(jnp.stack(jnp.split(update, lax.axis_size('ang'), axis=1))...  102 us
    all_to_all x1, waiting for transfers between devices, direct_path(): lax.all_to_all(grads, 'ang', split_axis=2, concat_axis=1, tiled=True)  84.6 us
    psum x1, blocking collectives, normalize(): totals = lax.psum(square_sums, ('ang', 'pix'))  70.5 us
    dot_general x5, matrix products, split_einsum(): jnp.einsum(form, left_piece, right_piece, preferred_element_type=jnp.floa...  56.7 us
    unnamed x83, local copies, waits for them, and re-layouts  28.7 us
    cos x1, other arithmetic, phase_pair(): return (jnp.cos(radians), jnp.sin(radians))  18 us
    all_to_all x1, starting transfers between devices, direct_path(): lax.all_to_all(grads, 'ang', split_axis=2, concat_axis=1, tiled=True)  11.2 us
  transfers between devices with their start and end apart: 1, of which 1 were waited for; matrix products, arithmetic and copies ran while one was open for 5% of the time, Pallas kernels for 0%

profile of v1, /device:TPU:1, one launch (start us, length us, event | category | flops | bytes accessed | tf_op | source)
XLA Modules:
  0.0 401.0 jit_solution(6046276937413356461)
XLA Ops:
  0.6 11.5 %copy.135 = bf16[2,64,64,512]{3,1,0,2:T(8,128)(2,1)} copy(bf16[2,64,64,512]{3,2,1,0:T(8,128)(2,1)} %param.4) | data formatting | bytes 16777216 | tf_op args[0]
  12.1 0.0 copy-start.6
  12.1 0.0 copy-start.8
  12.1 11.2 %all-to-all-start = ((bf16[2,64,64,512]{3,1,0,2:T(8,128)(2,1)}), bf16[2,64,64,512]{3,1,0,2:T(8,128)(2,1)}, u32[]{:S(2)}, u32[]{:S(2)}) async-start(bf16[2,64,64,512]{3,1,0,2:T(8,128)(2,1)} %copy.135), calls=%async_computation | async-start | bytes 16777216 | tf_op jit(solution)/shard_map/all_to_all | solution.py:44
  23.3 0.7 dynamic-slice_convert_fusion
  24.1 0.0 copy-done.6
  24.1 0.0 copy-done.8
  24.1 18.0 %fusion.8 = (f32[256,4096]{1,0:T(8,128)}, f32[256,4096]{1,0:T(8,128)}) fusion(s32[4096]{0:T(1024)S(1)} %copy-done.6, s32[256]{0:T(256)S(1)} %copy-done.8), kind=kLoop, calls=%fused_computation.23 | loop fusion | flops 14680064 | bytes 8406016 | tf_op jit(solution)/shard_map/cos | solution.py:10
  42.1 84.6 %all-to-all-done = bf16[2,64,64,512]{3,1,0,2:T(8,128)(2,1)} async-done(((bf16[2,64,64,512]{3,1,0,2:T(8,128)(2,1)}), bf16[2,64,64,512]{3,1,0,2:T(8,128)(2,1)}, u32[]{:S(2)}, u32[]{:S(2)}) %all-to-all-start) | async-done | bytes 8388640 | tf_op jit(solution)/shard_map/all_to_all | solution.py:44
  126.7 7.9 %copy.202 = bf16[2,64,64,512]{3,1,2,0:T(8,128)(2,1)} copy(bf16[2,64,64,512]{3,1,0,2:T(8,128)(2,1)} %all-to-all-done) | data formatting | bytes 16777216 | tf_op jit(solution)/shard_map/all_to_all | solution.py:44
  134.6 0.0 copy-start
  134.6 0.0 copy-start.2
  134.6 5.4 %fusion.27 = (bf16[1,64,64,1,512]{4,2,1,3,0:T(8,128)(2,1)S(1)}, bf16[1,64,64,1,512]{4,2,1,3,0:T(8,128)(2,1)}) fusion(bf16[2,64,64,1,512]{4,2,1,3,0:T(8,128)(2,1)} %bitcast.335), kind=kLoop, calls=%fused_computation.169 | loop fusion | bytes 16777216 | tf_op jit(solution)/shard_map/slice | solution.py:51
  140.0 0.0 copy-start.5
  140.0 2.1 copy-done.5
  142.1 0.0 copy-done
  142.1 1.5 copy-done.2
  143.6 8.0 %fusion.2 = f32[512,1024]{1,0:T(8,128)} fusion(bf16[4096,512]{1,0:T(8,128)(2,1)} %bitcast.339, bf16[4096,512]{1,0:T(8,128)(2,1)S(1)} %bitcast.337, f32[256,4096]{1,0:T(8,128)S(1)} %copy-done.2, f32[256,4096]{1,0:T(8,128)S(1)} %copy-done), kind=kOutput, calls=%fused_computation.15 | convolution fusion | flops 4322230272 | bytes 18874368 | tf_op jit(solution)/shard_map/ka,ap->kp/dot_general | solution.py:28
  151.6 8.5 %fusion.9 = f32[512,1024]{1,0:T(8,128)S(1)} fusion(f32[512,1024]{1,0:T(8,128)} %fusion.2, bf16[4096,512]{1,0:T(8,128)(2,1)} %bitcast.340, bf16[4096,512]{1,0:T(8,128)(2,1)} %bitcast.338, f32[256,4096]{1,0:T(8,128)S(1)} %copy-done.2, f32[256,4096]{1,0:T(8,128)S(1)} %copy-done), kind=kOutput, calls=%fused_computation.24 | convolution fusion | flops 4320657408 | bytes 20971520 | tf_op jit(solution)/shard_map/ka,ap->kp/dot_general | solution.py:28
  160.1 0.0 copy-start.4
  160.2 1.3 copy-done.4
  161.5 0.2 multiply_reduce_fusion
  161.7 70.5 %psum.7 = f32[256]{0:T(256)S(1)} all-reduce(f32[256]{0:T(256)S(1)} %multiply_reduce_fusion), channel_id=1, replica_groups=mesh['ang'=64,'pix'=2] {'ang','pix'}, use_global_device_ids=true, to_apply=%region_1.2 | all-reduce | flops 256 | bytes 2048 | tf_op jit(solution)/shard_map/psum | solution.py:35
  232.2 0.0 copy-start.7
  232.3 1.7 fusion.26
  234.0 0.0 copy-start.1
  234.0 0.0 copy-start.3
  234.0 12.7 %fusion.11 = f32[4096,1024]{1,0:T(8,128)} fusion(f32[256,512]{1,0:T(8,128)S(1)} %get-tuple-element.14, f32[256,512]{1,0:T(8,128)S(1)} %get-tuple-element.9, f32[256,512]{1,0:T(8,128)S(1)} %get-tuple-element.8, f32[256,4096]{1,0:T(8,128)} %get-tuple-element.16, f32[256,4096]{1,0:T(8,128)} %get-tuple-element.15), kind=kOutput, calls=%fused_computation.26 | convolution fusion | flops 4307025920 | bytes 26738688 | tf_op jit(solution)/shard_map/ka,kp->ap/dot_general | solution.py:28
  246.7 0.0 copy-done.7
  246.7 0.0 copy-done.1
  246.7 0.0 copy-done.3
  246.7 8.2 %fusion.19 = f32[4096,1024]{1,0:T(8,128)} fusion(f32[256,512]{1,0:T(8,128)S(1)} %get-tuple-element.14, f32[256,512]{1,0:T(8,128)S(1)} %get-tuple-element.9, f32[256,512]{1,0:T(8,128)S(1)} %get-tuple-element.8, f32[256,4096]{1,0:T(8,128)S(1)} %copy-done.3, f32[256,4096]{1,0:T(8,128)S(1)} %copy-done.1), kind=kOutput, calls=%fused_computation.167 | convolution fusion | flops 4307550208 | bytes 26738688 | tf_op jit(solution)/shard_map/ka,kp->ap/dot_general | solution.py:28
  254.9 19.3 %add_add_fusion = f32[4096,1024]{1,0:T(8,128)} fusion(f32[4096,1024]{1,0:T(8,128)} %fusion.19, f32[4096,1024]{1,0:T(8,128)} %fusion.11, f32[256,512]{1,0:T(8,128)S(1)} %get-tuple-element.14, f32[256,512]{1,0:T(8,128)S(1)} %get-tuple-element.9, f32[256,512]{1,0:T(8,128)S(1)} %get-tuple-element.8, f32[256,4096]{1,0:T(8,128)} %get-tuple-element.16, ...), kind=kOutput, calls=%fused_computation.2 | convolution fusion | flops 4318035968 | bytes 60293120 | tf_op jit(solution)/shard_map/ka,kp->ap/dot_general | solution.py:28
  274.1 6.9 %slice_bitcast_fusion.1 = (f32[1,4096,1,512]{3,1,2,0:T(8,128)S(1)}, f32[1,4096,1,512]{3,1,2,0:T(8,128)S(1)}) fusion(f32[4096,1024]{1,0:T(8,128)} %add_add_fusion), kind=kLoop, calls=%fused_computation.4 | loop fusion | bytes 33554432 | tf_op jit(solution)/shard_map/stack | solution.py:61
  281.0 2.5 fusion.28
  283.5 2.5 fusion
  287.3 102.3 %all_to_all.20 = bf16[64,2,64,1,512]{4,2,1,3,0:T(8,128)(2,1)} all-to-all(bf16[64,2,64,1,512]{4,2,1,3,0:T(8,128)(2,1)S(1)} %constant_dynamic-update-slice_fusion), channel_id=1, replica_groups=mesh['ang'=64,'pix'=2] {'ang'}, dimensions={0} | all-to-all | bytes 16777216 | tf_op jit(solution)/shard_map/all_to_all | solution.py:65
  389.5 11.5 %copy.200 = bf16[2,64,64,512]{3,2,1,0:T(8,128)(2,1)} copy(bf16[2,64,64,512]{3,1,0,2:T(8,128)(2,1)} %bitcast.336) | data formatting | bytes 16777216
  (65 shorter events, 0.7 us)
Async XLA Ops:
  12.1 11.9 %copy-start.6 = (s32[4096]{0:T(1024)S(1)}, s32[4096]{0:T(1024)}, u32[]{:S(2)}) copy-start(s32[4096]{0:T(1024)} %param.5) | copy-start | bytes 49156
  12.1 11.9 %copy-start.8 = (s32[256]{0:T(256)S(1)}, s32[256]{0:T(256)}, u32[]{:S(2)}) copy-start(s32[256]{0:T(256)} %param.6) | copy-start | bytes 3076
  12.1 114.6 %all-to-all-start = ((bf16[2,64,64,512]{3,1,0,2:T(8,128)(2,1)}), bf16[2,64,64,512]{3,1,0,2:T(8,128)(2,1)}, u32[]{:S(2)}, u32[]{:S(2)}) async-start(bf16[2,64,64,512]{3,1,0,2:T(8,128)(2,1)} %copy.135), calls=%async_computation | async-start | bytes 16777216 | tf_op jit(solution)/shard_map/all_to_all | solution.py:44
  134.6 7.5 %copy-start = (f32[256,4096]{1,0:T(8,128)S(1)}, f32[256,4096]{1,0:T(8,128)}, u32[]{:S(2)}) copy-start(f32[256,4096]{1,0:T(8,128)} %get-tuple-element.15) | copy-start | bytes 12582916
  134.6 9.0 %copy-start.2 = (f32[256,4096]{1,0:T(8,128)S(1)}, f32[256,4096]{1,0:T(8,128)}, u32[]{:S(2)}) copy-start(f32[256,4096]{1,0:T(8,128)} %get-tuple-element.16) | copy-start | bytes 12582916
  140.0 2.1 copy-start.5
  160.1 1.3 copy-start.4
  232.2 14.4 %copy-start.7 = (f32[256]{0:T(256)}, f32[256]{0:T(256)S(1)}, u32[]{:S(2)}) copy-start(f32[256]{0:T(256)S(1)} %add_sqrt_fusion) | copy-start | bytes 3076
  234.0 12.7 %copy-start.1 = (f32[256,4096]{1,0:T(8,128)S(1)}, f32[256,4096]{1,0:T(8,128)}, u32[]{:S(2)}) copy-start(f32[256,4096]{1,0:T(8,128)} %get-tuple-element.15) | copy-start | bytes 12582916
  234.0 12.7 %copy-start.3 = (f32[256,4096]{1,0:T(8,128)S(1)}, f32[256,4096]{1,0:T(8,128)}, u32[]{:S(2)}) copy-start(f32[256,4096]{1,0:T(8,128)} %get-tuple-element.16) | copy-start | bytes 12582916
